TPU v7x, 256 devices: a whole 4x4x8 slice. The times are simulated.
256 devices in a mesh: rows: 16 (over x, y), sub: 16 (over z, core).
Axes of the slice: x: 4, y: 4, z: 8, core: 2. Of those that a mesh axis runs over, the one named last changes fastest.
Arguments:
- embeddings: bfloat16 [65536, 1024], P(('rows', 'sub'))
- codes: int32 [64, 65536], P(None, ('rows', 'sub')), may hold values from 0 to 255
- codebook: bfloat16 [256, 1024], P(None, 'sub'), may hold values from -6 to 6
Outputs:
- rotation: float32 [1024, 1024], P('sub')
- rotated: bfloat16 [65536, 1024], P(('rows', 'sub'))
- new_codebook: float32 [256, 1024], P(None, 'sub')
All inputs are finite; a program needn't handle non-finite values.
Results may differ from a plain program's by a relative error of at most 0.0095.
Values may be sent and summed in bfloat16 or wider, within the bound.
No kernel may reach another device: no remote copies, remote signals or barrier semaphores. Data moves between devices by JAX's collectives and lax.ppermute only.
A program may use at most 64 MiB of HBM per device.

v0:
```python
import math
import jax
import jax.numpy as jnp
from jax import lax
from jax.sharding import PartitionSpec as P

NS_STEPS = 3
coef_a = 3.4445
coef_b = -4.775
coef_c = 2.0315
frob_eps = 1e-07
highest = lax.Precision.HIGHEST


def rows_dot(left, right):
    return lax.dot_general(
        left, right, (((1,), (1,)), ((), ())), precision=highest, preferred_element_type=jnp.float32
    )


def one_hot_codes(code_block, count_codes):
    levels = lax.broadcasted_iota(jnp.int32, code_block.shape + (count_codes,), 2)
    return (code_block[:, :, None] == levels).astype(jnp.bfloat16)


def decode_rows(codes, table):
    subspaces, local_rows = codes.shape
    count_codes, row_width = table.shape
    sub_width = row_width // subspaces
    block_rows = math.gcd(local_rows, 32768 // subspaces)
    blocks = local_rows // block_rows
    codewords = table.reshape(count_codes, subspaces, sub_width)
    code_blocks = codes.reshape(subspaces, blocks, block_rows).transpose(1, 0, 2)

    def decode_block(unused, code_block):
        one_hot = one_hot_codes(code_block, count_codes)
        picked = jnp.einsum("mnk,kmj->nmj", one_hot, codewords, preferred_element_type=jnp.float32)
        return (unused, picked.reshape(block_rows, row_width).astype(jnp.bfloat16))

    unused, decoded = lax.scan(decode_block, jnp.zeros((), jnp.float32), code_blocks)
    return decoded.reshape(local_rows, row_width)


def codeword_totals(codes, row_values, count_codes):
    subspaces, total_rows = codes.shape
    row_width = row_values.shape[1]
    sub_width = row_width // subspaces
    block_rows = math.gcd(total_rows, 32768 // subspaces)
    blocks = total_rows // block_rows
    code_blocks = codes.reshape(subspaces, blocks, block_rows).transpose(1, 0, 2)
    row_blocks = row_values.reshape(blocks, block_rows, subspaces, sub_width)

    def accumulate(running, pieces):
        one_hot = one_hot_codes(pieces[0], count_codes)
        block_sums = jnp.einsum(
            "mnk,nmj->kmj", one_hot, pieces[1], preferred_element_type=jnp.float32
        )
        block_counts = jnp.sum(one_hot, axis=1, dtype=jnp.float32).T
        return ((running[0] + block_sums, running[1] + block_counts), None)

    initial = (
        jnp.zeros((count_codes, subspaces, sub_width), jnp.float32),
        jnp.zeros((count_codes, subspaces), jnp.float32),
    )
    (code_sums, counts), unused = lax.scan(accumulate, initial, (code_blocks, row_blocks))
    return (code_sums.reshape(count_codes, row_width), counts)


def newton_panel(panel, whole):
    gram_rows = rows_dot(panel, whole)
    quartic = rows_dot(
        jnp.dot(gram_rows, whole, precision=highest, preferred_element_type=jnp.float32), whole
    )
    mixer = coef_b * gram_rows + coef_c * quartic
    return coef_a * panel + jnp.dot(
        mixer, whole, precision=highest, preferred_element_type=jnp.float32
    )


def collect(panel):
    return lax.all_gather(panel, "sub", axis=0, tiled=True)


def body(embeddings, codes, codebook):
    table = lax.all_gather(codebook, "sub", axis=1, tiled=True)
    decoded = decode_rows(codes, table)
    partial_panel = lax.psum_scatter(
        lax.dot_general(
            embeddings, decoded, (((0,), (0,)), ((), ())), preferred_element_type=jnp.float32
        ),
        "sub",
        scatter_dimension=0,
        tiled=True,
    )
    cross_panel = lax.psum(partial_panel, "rows")
    squares = lax.psum(jnp.sum(cross_panel * cross_panel), "sub")
    frob_scale = jnp.sqrt(squares) + frob_eps
    panel = cross_panel / frob_scale
    whole = collect(panel)
    for newton_step in range(NS_STEPS):
        if newton_step > 0:
            whole = collect(panel)
        panel = newton_panel(panel, whole)
    rotation_full = lax.all_gather(panel.astype(jnp.bfloat16), "sub", axis=0, tiled=True)
    rotated = jnp.dot(embeddings, rotation_full, preferred_element_type=jnp.float32).astype(
        jnp.bfloat16
    )
    moved_rows = lax.all_to_all(rotated, "sub", split_axis=1, concat_axis=0, tiled=True)
    moved_codes = lax.all_to_all(codes, "sub", split_axis=0, concat_axis=1, tiled=True)
    code_sums, counts = codeword_totals(moved_codes, moved_rows, table.shape[0])
    code_sums, counts = (
        lax.psum(code_sums.astype(jnp.bfloat16), "rows").astype(jnp.float32),
        lax.psum(counts.astype(jnp.bfloat16), "rows").astype(jnp.float32),
    )
    own_codebook = codebook.astype(jnp.float32)
    spread = jnp.repeat(counts, own_codebook.shape[1] // counts.shape[1], axis=1)
    new_codebook = (code_sums + own_codebook) / (spread + 1.0)
    return (panel, rotated, new_codebook)


def solution(mesh):
    in_specs = (P(("rows", "sub"), None), P(None, ("rows", "sub")), P(None, "sub"))
    out_specs = (P("sub", None), P(("rows", "sub"), None), P(None, "sub"))
    return jax.shard_map(body, mesh=mesh, in_specs=in_specs, out_specs=out_specs, check_vma=False)
```

profile of v0, /device:TPU:64, one launch (start us, length us, event | category | flops | bytes accessed | tf_op | source)
XLA Modules:
  0.0 547.7 jit_solution(3402713358330620616)
XLA Ops:
  7.2 0.0 copy-start
  7.2 0.0 reduce-scatter.4.cloned.1.call-start
  7.2 18.8 %all_gather.15 = bf16[256,1024]{0,1:T(8,128)(2,1)S(1)} all-gather(bf16[256,64]{0,1:T(8,128)(2,1)} %param.5), channel_id=1, replica_groups=mesh['rows'=16,'sub'=16] {'sub'}, dimensions={1}, use_global_device_ids=true | all-gather | bytes 557056 | tf_op jit(solution)/shard_map/all_gather | solution.py:85
  26.0 5.3 fusion.6
  31.3 0.0 copy-done
  31.3 2.7 convolution_bitcast_fusion
  34.0 5.4 copy.15
  39.3 0.0 reduce-scatter.4.cloned.1.call-update
  39.4 0.0 all-reduce.3.cloned.1.call-start
  39.4 58.3 %reduce-scatter.4.cloned.1.call-done = f32[64,1024]{1,0:T(8,128)} async-done(((f32[1024,1024]{1,0:T(8,128)}), f32[64,1024]{1,0:T(8,128)}) %reduce-scatter.4.cloned.1.call-update) | async-done | bytes 262160 | tf_op jit(solution)/shard_map/reduce_scatter | solution.py:87
  97.7 0.0 all-reduce.3.cloned.1.call-update
  97.7 0.0 all-gather.5.cloned.1.call-start
  97.8 102.1 %all-reduce.3.cloned.1.call-done = f32[64,1024]{1,0:T(8,128)} async-done(((f32[64,1024]{1,0:T(8,128)}), f32[64,1024]{1,0:T(8,128)}) %all-reduce.3.cloned.1.call-update) | async-done | bytes 262160 | tf_op jit(solution)/shard_map/psum | solution.py:95
  199.9 1.6 multiply_reduce_fusion
  201.5 21.1 %psum.29 = f32[]{:T(128)} all-reduce(f32[]{:T(128)} %multiply_reduce_fusion), channel_id=1, replica_groups=mesh['rows'=16,'sub'=16] {'sub'}, use_global_device_ids=true, to_apply=%region_3.4 | all-reduce | flops 1 | bytes 8 | tf_op jit(solution)/shard_map/psum | solution.py:96
  223.3 1.7 broadcast_divide_fusion
  224.9 0.0 all-gather.5.cloned.1.call-update
  225.0 0.0 all-gather.7.cloned.1.call-start
  225.0 43.2 %all-gather.5.cloned.1.call-done = f32[1024,1024]{1,0:T(8,128)} async-done(((f32[64,1024]{1,0:T(8,128)}), f32[1024,1024]{1,0:T(8,128)}) %all-gather.5.cloned.1.call-update) | async-done | bytes 4194320 | tf_op jit(solution)/shard_map/all_gather | solution.py:81
  268.2 6.5 %fusion.12 = f32[64,1024]{1,0:T(8,128)S(1)} fusion(f32[64,1024]{1,0:T(8,128)} %broadcast_divide_fusion, f32[1024,1024]{1,0:T(8,128)} %all-gather.5.cloned.1.call-done), kind=kOutput, calls=%fused_computation.26 | convolution fusion | flops 805306368 | bytes 4718592 | tf_op jit(solution)/shard_map/dot_general | solution.py:16
  274.7 0.0 copy-done.2
  274.7 0.0 copy-start.6
  274.8 2.6 fusion.13
  277.4 4.2 fusion.9
  281.6 0.0 copy-done.6
  281.6 3.4 convolution_add_fusion.2
  284.9 0.0 all-gather.7.cloned.1.call-update
  285.0 0.5 all-gather.9.cloned.1.call-start
  285.5 40.1 %all-gather.7.cloned.1.call-done = f32[1024,1024]{1,0:T(8,128)} async-done(((f32[64,1024]{1,0:T(8,128)}), f32[1024,1024]{1,0:T(8,128)}) %all-gather.7.cloned.1.call-update) | async-done | bytes 4194320 | tf_op jit(solution)/shard_map/all_gather | solution.py:81
  325.5 6.5 %fusion.14 = f32[64,1024]{1,0:T(8,128)S(1)} fusion(f32[64,1024]{1,0:T(8,128)} %convolution_add_fusion.2, f32[1024,1024]{1,0:T(8,128)} %all-gather.7.cloned.1.call-done), kind=kOutput, calls=%fused_computation.28 | convolution fusion | flops 805306368 | bytes 4718592 | tf_op jit(solution)/shard_map/dot_general | solution.py:16
  332.0 0.0 copy-done.3
  332.0 0.0 copy-start.5
  332.0 2.6 fusion.15
  334.7 4.2 fusion.8
  338.9 0.0 copy-done.5
  338.9 3.4 convolution_add_fusion.1
  342.2 0.0 all-gather.9.cloned.1.call-update
  342.2 0.2 all-gather.11.cloned.1.call-start
  342.5 40.4 %all-gather.9.cloned.1.call-done = f32[1024,1024]{1,0:T(8,128)} async-done(((f32[64,1024]{1,0:T(8,128)}), f32[1024,1024]{1,0:T(8,128)}) %all-gather.9.cloned.1.call-update) | async-done | bytes 4194320 | tf_op jit(solution)/shard_map/all_gather | solution.py:81
  382.8 6.5 %fusion.16 = f32[64,1024]{1,0:T(8,128)S(1)} fusion(f32[64,1024]{1,0:T(8,128)} %convolution_add_fusion.1, f32[1024,1024]{1,0:T(8,128)} %all-gather.9.cloned.1.call-done), kind=kOutput, calls=%fused_computation.30 | convolution fusion | flops 805306368 | bytes 4718592 | tf_op jit(solution)/shard_map/dot_general | solution.py:16
  389.3 0.0 copy-done.1
  389.3 0.0 copy-start.4
  389.3 2.7 fusion.17
  392.0 0.0 copy-start.8
  392.0 4.2 fusion.7
  396.2 0.0 copy-done.4
  396.2 3.4 fusion.11
  399.6 0.0 all-gather.11.cloned.1.call-update
  399.6 0.0 copy-done.8
  399.6 0.7 all_to_all.27
  400.3 6.0 %all-to-all-start.1 = ((s32[16,4,256]{2,1,0:T(4,128)}), s32[16,4,256]{2,1,0:T(4,128)S(1)}, u32[]{:S(2)}, u32[]{:S(2)}) async-start(s32[16,4,256]{2,1,0:T(4,128)} %all_to_all.27), calls=%async_computation.1 | async-start | bytes 131072 | tf_op jit(solution)/shard_map/all_to_all | solution.py:109
  406.3 31.3 %all-gather.11.cloned.1.call-done = bf16[1024,1024]{1,0:T(8,128)(2,1)} async-done(((bf16[64,1024]{1,0:T(8,128)(2,1)}), bf16[1024,1024]{1,0:T(8,128)(2,1)}) %all-gather.11.cloned.1.call-update) | async-done | bytes 2097168 | tf_op jit(solution)/shard_map/all_gather | solution.py:104
  437.6 3.2 convolution_convert_fusion
  440.8 0.0 all-to-all-done.1
  440.8 6.4 %all-to-all-start = ((bf16[256,16,64]{0,2,1:T(8,128)(2,1)}), bf16[256,16,64]{0,2,1:T(8,128)(2,1)S(1)}, u32[]{:S(2)}, u32[]{:S(2)}) async-start(bf16[256,16,64]{0,2,1:T(8,128)(2,1)} %bitcast.5), calls=%async_computation | async-start | bytes 1048576 | tf_op jit(solution)/shard_map/all_to_all | solution.py:108
  447.1 6.9 %fusion.3 = bf16[4,256]{1,0:T(4,128)(2,1)S(1)} fusion(s32[4,4096]{1,0:T(4,128)S(1)} %bitcast.55), kind=kLoop, calls=%fused_computation.5 | loop fusion | flops 12581888 | bytes 67584 | tf_op jit(solution)/shard_map/while/body/eval_jaxpr/reduce_sum | solution.py:58
  454.1 2.0 copy.14
  456.1 5.9 %all-to-all-done = bf16[256,16,64]{0,2,1:T(8,128)(2,1)S(1)} async-done(((bf16[256,16,64]{0,2,1:T(8,128)(2,1)}), bf16[256,16,64]{0,2,1:T(8,128)(2,1)S(1)}, u32[]{:S(2)}, u32[]{:S(2)}) %all-to-all-start) | async-done | bytes 524320 | tf_op jit(solution)/shard_map/all_to_all | solution.py:108
  462.0 0.3 copy.13
  462.3 0.2 squeeze.11
  462.5 3.2 fusion.10
  465.8 74.2 %all-reduce = (bf16[256,64]{0,1:T(8,128)(2,1)S(1)}, bf16[256,4]{0,1:T(4,128)(2,1)S(1)}) all-reduce(bf16[256,64]{0,1:T(8,128)(2,1)S(1)} %bitcast.57, bf16[256,4]{0,1:T(4,128)(2,1)S(1)} %bitcast.58), channel_id=1, replica_groups=mesh['rows'=16,'sub'=16] {'rows'}, use_global_device_ids=true, to_apply=%region_4.5 | all-reduce | flops 17408 | bytes 69632 | tf_op jit(solution)/shard_map/psum | solution.py:112
  540.0 0.0 copy-done.7
  540.0 0.6 bitcast_divide_fusion
  (5 shorter events, 0.0 us)
Async XLA Ops:
  7.2 24.1 %copy-start = (bf16[256,1024]{1,0:T(8,128)(2,1)S(1)}, bf16[256,1024]{1,0:T(8,128)(2,1)}, u32[]{:S(2)}) copy-start(bf16[256,1024]{1,0:T(8,128)(2,1)} %param.3) | copy-start | bytes 1572868
  7.2 90.5 %reduce-scatter.4.cloned.1.call-start = ((), (), s32[]{:S(2)}) async-start(), calls=%async_computation.8 | async-start | bytes 4456448 | tf_op jit(solution)/shard_map/reduce_scatter | solution.py:87
  39.4 160.5 %all-reduce.3.cloned.1.call-start = ((), (), s32[]{:S(2)}) async-start(), calls=%async_computation.3 | async-start | bytes 524288 | tf_op jit(solution)/shard_map/psum | solution.py:95
  97.7 170.5 %all-gather.5.cloned.1.call-start = ((), (), s32[]{:S(2)}) async-start(), calls=%async_computation.4 | async-start | bytes 4456448 | tf_op jit(solution)/shard_map/all_gather | solution.py:81
  225.0 100.6 %all-gather.7.cloned.1.call-start = ((), (), s32[]{:S(2)}) async-start(), calls=%async_computation.5 | async-start | bytes 4456448 | tf_op jit(solution)/shard_map/all_gather | solution.py:81
  268.2 6.5 %copy-start.2 = (f32[1024,1024]{1,0:T(8,128)S(1)}, f32[1024,1024]{1,0:T(8,128)}, u32[]{:S(2)}) copy-start(f32[1024,1024]{1,0:T(8,128)} %all-gather.5.cloned.1.call-done) | copy-start | bytes 12582916
  274.7 6.8 %copy-start.6 = (f32[64,1024]{1,0:T(8,128)S(1)}, f32[64,1024]{1,0:T(8,128)}, u32[]{:S(2)}) copy-start(f32[64,1024]{1,0:T(8,128)} %broadcast_divide_fusion) | copy-start | bytes 786436
  285.0 97.9 %all-gather.9.cloned.1.call-start = ((), (), s32[]{:S(2)}) async-start(), calls=%async_computation.6 | async-start | bytes 4456448 | tf_op jit(solution)/shard_map/all_gather | solution.py:81
  325.5 6.5 %copy-start.3 = (f32[1024,1024]{1,0:T(8,128)S(1)}, f32[1024,1024]{1,0:T(8,128)}, u32[]{:S(2)}) copy-start(f32[1024,1024]{1,0:T(8,128)} %all-gather.7.cloned.1.call-done) | copy-start | bytes 12582916
  332.0 6.8 %copy-start.5 = (f32[64,1024]{1,0:T(8,128)S(1)}, f32[64,1024]{1,0:T(8,128)}, u32[]{:S(2)}) copy-start(f32[64,1024]{1,0:T(8,128)} %convolution_add_fusion.2) | copy-start | bytes 786436
  342.2 95.4 %all-gather.11.cloned.1.call-start = ((), (), s32[]{:S(2)}) async-start(), calls=%async_computation.7 | async-start | bytes 2228224 | tf_op jit(solution)/shard_map/all_gather | solution.py:104
  382.8 6.5 %copy-start.1 = (f32[1024,1024]{1,0:T(8,128)S(1)}, f32[1024,1024]{1,0:T(8,128)}, u32[]{:S(2)}) copy-start(f32[1024,1024]{1,0:T(8,128)} %all-gather.9.cloned.1.call-done) | copy-start | bytes 12582916
  389.3 6.9 %copy-start.4 = (f32[64,1024]{1,0:T(8,128)S(1)}, f32[64,1024]{1,0:T(8,128)}, u32[]{:S(2)}) copy-start(f32[64,1024]{1,0:T(8,128)} %convolution_add_fusion.1) | copy-start | bytes 786436
  392.0 7.6 %copy-start.8 = (s32[64,256]{1,0:T(8,128)S(1)}, s32[64,256]{1,0:T(8,128)}, u32[]{:S(2)}) copy-start(s32[64,256]{1,0:T(8,128)} %param.4) | copy-start | bytes 196612
  400.3 40.5 %all-to-all-start.1 = ((s32[16,4,256]{2,1,0:T(4,128)}), s32[16,4,256]{2,1,0:T(4,128)S(1)}, u32[]{:S(2)}, u32[]{:S(2)}) async-start(s32[16,4,256]{2,1,0:T(4,128)} %all_to_all.27), calls=%async_computation.1 | async-start | bytes 131072 | tf_op jit(solution)/shard_map/all_to_all | solution.py:109
  440.8 21.2 %all-to-all-start = ((bf16[256,16,64]{0,2,1:T(8,128)(2,1)}), bf16[256,16,64]{0,2,1:T(8,128)(2,1)S(1)}, u32[]{:S(2)}, u32[]{:S(2)}) async-start(bf16[256,16,64]{0,2,1:T(8,128)(2,1)} %bitcast.5), calls=%async_computation | async-start | bytes 1048576 | tf_op jit(solution)/shard_map/all_to_all | solution.py:108
  456.1 83.9 %copy-start.7 = (bf16[256,64]{0,1:T(8,128)(2,1)S(1)}, bf16[256,64]{0,1:T(8,128)(2,1)}, u32[]{:S(2)}) copy-start(bf16[256,64]{0,1:T(8,128)(2,1)} %param.5) | copy-start | bytes 98308
Sparse Core Ops, SparseCore 0:
  39.5 58.1 reduce-scatter.3
  100.9 98.9 all-reduce.2
  225.1 43.1 all-gather.4
  285.1 40.4 all-gather.6
  342.4 40.4 all-gather.8
  399.7 37.8 all-gather.10
where the time goes:
time: 557 us; the launch traced here: 548 us
  waiting for transfers between devices  321 us (58%)
  blocking collectives  114 us (20%)
  matrix products  64.3 us (12%)
  between operations  15.2 us (3%)
  starting transfers between devices  13.3 us (2%)
  other arithmetic  10.9 us (2%)
  local copies, waits for them, and re-layouts  8.64 us (2%)
    all_gather x3, waiting for transfers between devices, collect(): return lax.all_gather(panel, 'sub', axis=0, tiled=True)  124 us
    psum x1, waiting for transfers between devices, body(): cross_panel = lax.psum(partial_panel, 'rows')  102 us
    psum x1, blocking collectives, body(): lax.psum(code_sums.astype(jnp.bfloat16), 'rows').astype(jnp.float32)  74.2 us
    reduce_scatter x1, waiting for transfers between devices, body(): lax.psum_scatter(lax.dot_general(embeddings, decoded, (((0,), (0,)), ((),...  58.3 us
    dot_general x6, matrix products, rows_dot(): lax.dot_general(left, right, (((1,), (1,)), ((), ())), precision=highest,...  31.9 us
    all_gather x1, waiting for transfers between devices, body(): lax.all_gather(panel.astype(jnp.bfloat16), 'sub', axis=0, tiled=True)  31.3 us
    psum x1, blocking collectives, body(): squares = lax.psum(jnp.sum(cross_panel * cross_panel), 'sub')  21.1 us
    all_gather x1, blocking collectives, body(): table = lax.all_gather(codebook, 'sub', axis=1, tiled=True)  18.8 us
  transfers between devices with their start and end apart: 8, of which 7 were waited for; matrix products, arithmetic and copies ran while one was open for 2% of the time, Pallas kernels for 0%

commit v1 on v0

--- a/solution.py
+++ b/solution.py
@@ -92,7 +92,7 @@
         scatter_dimension=0,
         tiled=True,
     )
-    cross_panel = lax.psum(partial_panel, "rows")
+    cross_panel = jnp.sum(lax.all_gather(partial_panel, "rows"), axis=0)
     squares = lax.psum(jnp.sum(cross_panel * cross_panel), "sub")
     frob_scale = jnp.sqrt(squares) + frob_eps
     panel = cross_panel / frob_scale

time: 557 us -> 512 us (0.919); the launches traced: 548 us -> 509 us
  waiting for transfers between devices: 321 us -> 282 us
    psum x1 -> x0, waiting for transfers between devices: 102 us -> none  [body(): cross_panel = lax.psum(partial_panel, 'rows')]
    all_gather x0 -> x1, waiting for transfers between devices: none -> 62.8 us  [body(): cross_panel = jnp.sum(lax.all_gather(partial_panel, 'rows'), axis=0)]
where the time goes in v1:
time: 512 us; the launch traced here: 509 us
  waiting for transfers between devices  282 us (55%)
  blocking collectives  114 us (22%)
  matrix products  64.3 us (13%)
  between operations  15.2 us (3%)
  starting transfers between devices  13.6 us (3%)
  other arithmetic  11.4 us (2%)
  local copies, waits for them, and re-layouts  8.64 us (2%)
    all_gather x3, waiting for transfers between devices, collect(): return lax.all_gather(panel, 'sub', axis=0, tiled=True)  124 us
    psum x1, blocking collectives, body(): lax.psum(code_sums.astype(jnp.bfloat16), 'rows').astype(jnp.float32)  74.2 us
    all_gather x1, waiting for transfers between devices, body(): cross_panel = jnp.sum(lax.all_gather(partial_panel, 'rows'), axis=0)  62.8 us
    reduce_scatter x1, waiting for transfers between devices, body(): lax.psum_scatter(lax.dot_general(embeddings, decoded, (((0,), (0,)), ((),...  58.3 us
    dot_general x6, matrix products, rows_dot(): lax.dot_general(left, right, (((1,), (1,)), ((), ())), precision=highest,...  31.9 us
    all_gather x1, waiting for transfers between devices, body(): lax.all_gather(panel.astype(jnp.bfloat16), 'sub', axis=0, tiled=True)  31.3 us
    psum x1, blocking collectives, body(): squares = lax.psum(jnp.sum(cross_panel * cross_panel), 'sub')  21.1 us
    all_gather x1, blocking collectives, body(): table = lax.all_gather(codebook, 'sub', axis=1, tiled=True)  18.8 us
  transfers between devices with their start and end apart: 8, of which 7 were waited for; matrix products, arithmetic and copies ran while one was open for 2% of the time, Pallas kernels for 0%

profile of v1, /device:TPU:64, one launch (start us, length us, event | category | flops | bytes accessed | tf_op | source)
XLA Modules:
  0.0 509.3 jit_solution(17758776921306405221)
XLA Ops:
  7.2 0.0 copy-start
  7.2 0.0 reduce-scatter.4.cloned.1.call-start
  7.2 18.8 %all_gather.21 = bf16[256,1024]{0,1:T(8,128)(2,1)S(1)} all-gather(bf16[256,64]{0,1:T(8,128)(2,1)} %param.5), channel_id=1, replica_groups=mesh['rows'=16,'sub'=16] {'sub'}, dimensions={1}, use_global_device_ids=true | all-gather | bytes 557056 | tf_op jit(solution)/shard_map/all_gather | solution.py:85
  26.0 5.3 %fusion.6 = bf16[64,256,16]{1,2,0:T(8,128)(2,1)S(1)} fusion(bf16[256,64,16]{0,2,1:T(8,128)(2,1)S(1)} %bitcast.56, s32[64,256]{1,0:T(8,128)} %param.4), kind=kOutput, calls=%fused_computation.9 | convolution fusion | flops 138674176 | bytes 1114112 | tf_op jit(solution)/shard_map/while/body/eval_jaxpr/mnk,kmj->nmj/dot_general | solution.py:37
  31.3 0.0 copy-done
  31.3 2.7 convolution_bitcast_fusion
  34.0 5.4 %copy.14 = f32[1024,1024]{1,0:T(8,128)} copy(f32[1024,1024]{0,1:T(8,128)} %convolution_bitcast_fusion) | data formatting | bytes 8388608
  39.3 0.0 reduce-scatter.4.cloned.1.call-update
  39.4 0.0 all-gather.15.cloned.1.call-start
  39.4 58.3 %reduce-scatter.4.cloned.1.call-done = f32[64,1024]{1,0:T(8,128)} async-done(((f32[1024,1024]{1,0:T(8,128)}), f32[64,1024]{1,0:T(8,128)}) %reduce-scatter.4.cloned.1.call-update) | async-done | bytes 262160 | tf_op jit(solution)/shard_map/reduce_scatter | solution.py:87
  97.7 0.0 all-gather.15.cloned.1.call-update
  97.7 0.0 all-gather.7.cloned.1.call-start
  97.8 62.8 %all-gather.15.cloned.1.call-done = f32[1024,1024]{1,0:T(8,128)} async-done(((f32[64,1024]{1,0:T(8,128)}), f32[1024,1024]{1,0:T(8,128)}) %all-gather.15.cloned.1.call-update) | async-done | bytes 4194320 | tf_op jit(solution)/shard_map/all_gather | solution.py:95
  160.6 2.5 reduce_sum.31
  163.1 0.7 multiply_reduce_fusion
  163.7 21.1 %psum.21 = f32[]{:T(128)} all-reduce(f32[]{:T(128)} %multiply_reduce_fusion), channel_id=1, replica_groups=mesh['rows'=16,'sub'=16] {'sub'}, use_global_device_ids=true, to_apply=%region_3.4 | all-reduce | flops 1 | bytes 8 | tf_op jit(solution)/shard_map/psum | solution.py:96
  185.5 0.7 broadcast_divide_fusion
  186.2 0.0 all-gather.7.cloned.1.call-update
  186.3 0.3 all-gather.9.cloned.1.call-start
  186.6 43.2 %all-gather.7.cloned.1.call-done = f32[1024,1024]{1,0:T(8,128)} async-done(((f32[64,1024]{1,0:T(8,128)}), f32[1024,1024]{1,0:T(8,128)}) %all-gather.7.cloned.1.call-update) | async-done | bytes 4194320 | tf_op jit(solution)/shard_map/all_gather | solution.py:81
  229.8 6.5 %fusion.12 = f32[64,1024]{1,0:T(8,128)S(1)} fusion(f32[64,1024]{1,0:T(8,128)} %broadcast_divide_fusion, f32[1024,1024]{1,0:T(8,128)} %all-gather.7.cloned.1.call-done), kind=kOutput, calls=%fused_computation.26 | convolution fusion | flops 805306368 | bytes 4718592 | tf_op jit(solution)/shard_map/dot_general | solution.py:16
  236.3 0.0 copy-done.2
  236.3 0.0 copy-start.6
  236.3 2.6 fusion.13
  238.9 4.2 fusion.9
  243.1 0.0 copy-done.6
  243.1 3.4 convolution_add_fusion.2
  246.5 0.0 all-gather.9.cloned.1.call-update
  246.5 0.6 all-gather.11.cloned.1.call-start
  247.1 40.0 %all-gather.9.cloned.1.call-done = f32[1024,1024]{1,0:T(8,128)} async-done(((f32[64,1024]{1,0:T(8,128)}), f32[1024,1024]{1,0:T(8,128)}) %all-gather.9.cloned.1.call-update) | async-done | bytes 4194320 | tf_op jit(solution)/shard_map/all_gather | solution.py:81
  287.1 6.5 %fusion.14 = f32[64,1024]{1,0:T(8,128)S(1)} fusion(f32[64,1024]{1,0:T(8,128)} %convolution_add_fusion.2, f32[1024,1024]{1,0:T(8,128)} %all-gather.9.cloned.1.call-done), kind=kOutput, calls=%fused_computation.28 | convolution fusion | flops 805306368 | bytes 4718592 | tf_op jit(solution)/shard_map/dot_general | solution.py:16
  293.6 0.0 copy-done.3
  293.6 0.0 copy-start.5
  293.6 2.6 fusion.15
  296.2 4.2 fusion.8
  300.4 0.0 copy-done.5
  300.4 3.4 convolution_add_fusion.1
  303.7 0.0 all-gather.11.cloned.1.call-update
  303.8 0.2 all-gather.13.cloned.1.call-start
  304.0 40.4 %all-gather.11.cloned.1.call-done = f32[1024,1024]{1,0:T(8,128)} async-done(((f32[64,1024]{1,0:T(8,128)}), f32[1024,1024]{1,0:T(8,128)}) %all-gather.11.cloned.1.call-update) | async-done | bytes 4194320 | tf_op jit(solution)/shard_map/all_gather | solution.py:81
  344.4 6.5 %fusion.16 = f32[64,1024]{1,0:T(8,128)S(1)} fusion(f32[64,1024]{1,0:T(8,128)} %convolution_add_fusion.1, f32[1024,1024]{1,0:T(8,128)} %all-gather.11.cloned.1.call-done), kind=kOutput, calls=%fused_computation.30 | convolution fusion | flops 805306368 | bytes 4718592 | tf_op jit(solution)/shard_map/dot_general | solution.py:16
  350.9 0.0 copy-done.1
  350.9 0.0 copy-start.4
  350.9 2.7 fusion.17
  353.5 0.0 copy-start.8
  353.5 4.2 fusion.7
  357.7 0.0 copy-done.4
  357.7 3.4 fusion.11
  361.1 0.0 all-gather.13.cloned.1.call-update
  361.2 0.0 copy-done.8
  361.2 0.7 all_to_all.27
  361.8 6.0 %all-to-all-start.1 = ((s32[16,4,256]{2,1,0:T(4,128)}), s32[16,4,256]{2,1,0:T(4,128)S(1)}, u32[]{:S(2)}, u32[]{:S(2)}) async-start(s32[16,4,256]{2,1,0:T(4,128)} %all_to_all.27), calls=%async_computation.1 | async-start | bytes 131072 | tf_op jit(solution)/shard_map/all_to_all | solution.py:109
  367.8 31.3 %all-gather.13.cloned.1.call-done = bf16[1024,1024]{1,0:T(8,128)(2,1)} async-done(((bf16[64,1024]{1,0:T(8,128)(2,1)}), bf16[1024,1024]{1,0:T(8,128)(2,1)}) %all-gather.13.cloned.1.call-update) | async-done | bytes 2097168 | tf_op jit(solution)/shard_map/all_gather | solution.py:104
  399.1 3.2 convolution_convert_fusion
  402.3 0.0 all-to-all-done.1
  402.3 6.4 %all-to-all-start = ((bf16[256,16,64]{0,2,1:T(8,128)(2,1)}), bf16[256,16,64]{0,2,1:T(8,128)(2,1)S(1)}, u32[]{:S(2)}, u32[]{:S(2)}) async-start(bf16[256,16,64]{0,2,1:T(8,128)(2,1)} %bitcast.6), calls=%async_computation | async-start | bytes 1048576 | tf_op jit(solution)/shard_map/all_to_all | solution.py:108
  408.7 6.9 %fusion.3 = bf16[4,256]{1,0:T(4,128)(2,1)S(1)} fusion(s32[4,4096]{1,0:T(4,128)S(1)} %bitcast.57), kind=kLoop, calls=%fused_computation.5 | loop fusion | flops 12581888 | bytes 67584 | tf_op jit(solution)/shard_map/while/body/eval_jaxpr/reduce_sum | solution.py:58
  415.6 2.0 copy.13
  417.6 5.9 %all-to-all-done = bf16[256,16,64]{0,2,1:T(8,128)(2,1)S(1)} async-done(((bf16[256,16,64]{0,2,1:T(8,128)(2,1)}), bf16[256,16,64]{0,2,1:T(8,128)(2,1)S(1)}, u32[]{:S(2)}, u32[]{:S(2)}) %all-to-all-start) | async-done | bytes 524320 | tf_op jit(solution)/shard_map/all_to_all | solution.py:108
  423.5 0.3 copy.12
  423.8 0.2 squeeze.11
  424.1 3.2 fusion.10
  427.3 74.2 %all-reduce = (bf16[256,64]{0,1:T(8,128)(2,1)S(1)}, bf16[256,4]{0,1:T(4,128)(2,1)S(1)}) all-reduce(bf16[256,64]{0,1:T(8,128)(2,1)S(1)} %bitcast.59, bf16[256,4]{0,1:T(4,128)(2,1)S(1)} %bitcast.60), channel_id=1, replica_groups=mesh['rows'=16,'sub'=16] {'rows'}, use_global_device_ids=true, to_apply=%region_4.5 | all-reduce | flops 17408 | bytes 69632 | tf_op jit(solution)/shard_map/psum | solution.py:112
  501.5 0.6 bitcast_divide_fusion
  (6 shorter events, 0.0 us)
Async XLA Ops:
  7.2 24.1 %copy-start = (bf16[256,1024]{1,0:T(8,128)(2,1)S(1)}, bf16[256,1024]{1,0:T(8,128)(2,1)}, u32[]{:S(2)}) copy-start(bf16[256,1024]{1,0:T(8,128)(2,1)} %param.3) | copy-start | bytes 1572868
  7.2 90.5 %reduce-scatter.4.cloned.1.call-start = ((), (), s32[]{:S(2)}) async-start(), calls=%async_computation.8 | async-start | bytes 4456448 | tf_op jit(solution)/shard_map/reduce_scatter | solution.py:87
  39.4 121.2 %all-gather.15.cloned.1.call-start = ((), (), s32[]{:S(2)}) async-start(), calls=%async_computation.7 | async-start | bytes 4456448 | tf_op jit(solution)/shard_map/all_gather | solution.py:95
  97.7 132.1 %all-gather.7.cloned.1.call-start = ((), (), s32[]{:S(2)}) async-start(), calls=%async_computation.3 | async-start | bytes 4456448 | tf_op jit(solution)/shard_map/all_gather | solution.py:81
  186.3 100.8 %all-gather.9.cloned.1.call-start = ((), (), s32[]{:S(2)}) async-start(), calls=%async_computation.4 | async-start | bytes 4456448 | tf_op jit(solution)/shard_map/all_gather | solution.py:81
  229.8 6.5 %copy-start.2 = (f32[1024,1024]{1,0:T(8,128)S(1)}, f32[1024,1024]{1,0:T(8,128)}, u32[]{:S(2)}) copy-start(f32[1024,1024]{1,0:T(8,128)} %all-gather.7.cloned.1.call-done) | copy-start | bytes 12582916
  236.3 6.8 %copy-start.6 = (f32[64,1024]{1,0:T(8,128)S(1)}, f32[64,1024]{1,0:T(8,128)}, u32[]{:S(2)}) copy-start(f32[64,1024]{1,0:T(8,128)} %broadcast_divide_fusion) | copy-start | bytes 786436
  246.5 97.9 %all-gather.11.cloned.1.call-start = ((), (), s32[]{:S(2)}) async-start(), calls=%async_computation.5 | async-start | bytes 4456448 | tf_op jit(solution)/shard_map/all_gather | solution.py:81
  287.1 6.5 %copy-start.3 = (f32[1024,1024]{1,0:T(8,128)S(1)}, f32[1024,1024]{1,0:T(8,128)}, u32[]{:S(2)}) copy-start(f32[1024,1024]{1,0:T(8,128)} %all-gather.9.cloned.1.call-done) | copy-start | bytes 12582916
  293.6 6.8 %copy-start.5 = (f32[64,1024]{1,0:T(8,128)S(1)}, f32[64,1024]{1,0:T(8,128)}, u32[]{:S(2)}) copy-start(f32[64,1024]{1,0:T(8,128)} %convolution_add_fusion.2) | copy-start | bytes 786436
  303.8 95.4 %all-gather.13.cloned.1.call-start = ((), (), s32[]{:S(2)}) async-start(), calls=%async_computation.6 | async-start | bytes 2228224 | tf_op jit(solution)/shard_map/all_gather | solution.py:104
  344.4 6.5 %copy-start.1 = (f32[1024,1024]{1,0:T(8,128)S(1)}, f32[1024,1024]{1,0:T(8,128)}, u32[]{:S(2)}) copy-start(f32[1024,1024]{1,0:T(8,128)} %all-gather.11.cloned.1.call-done) | copy-start | bytes 12582916
  350.9 6.9 %copy-start.4 = (f32[64,1024]{1,0:T(8,128)S(1)}, f32[64,1024]{1,0:T(8,128)}, u32[]{:S(2)}) copy-start(f32[64,1024]{1,0:T(8,128)} %convolution_add_fusion.1) | copy-start | bytes 786436
  353.5 7.6 %copy-start.8 = (s32[64,256]{1,0:T(8,128)S(1)}, s32[64,256]{1,0:T(8,128)}, u32[]{:S(2)}) copy-start(s32[64,256]{1,0:T(8,128)} %param.4) | copy-start | bytes 196612
  361.8 40.5 %all-to-all-start.1 = ((s32[16,4,256]{2,1,0:T(4,128)}), s32[16,4,256]{2,1,0:T(4,128)S(1)}, u32[]{:S(2)}, u32[]{:S(2)}) async-start(s32[16,4,256]{2,1,0:T(4,128)} %all_to_all.27), calls=%async_computation.1 | async-start | bytes 131072 | tf_op jit(solution)/shard_map/all_to_all | solution.py:109
  402.3 21.2 %all-to-all-start = ((bf16[256,16,64]{0,2,1:T(8,128)(2,1)}), bf16[256,16,64]{0,2,1:T(8,128)(2,1)S(1)}, u32[]{:S(2)}, u32[]{:S(2)}) async-start(bf16[256,16,64]{0,2,1:T(8,128)(2,1)} %bitcast.6), calls=%async_computation | async-start | bytes 1048576 | tf_op jit(solution)/shard_map/all_to_all | solution.py:108
  417.6 83.9 %copy-start.7 = (bf16[256,64]{0,1:T(8,128)(2,1)S(1)}, bf16[256,64]{0,1:T(8,128)(2,1)}, u32[]{:S(2)}) copy-start(bf16[256,64]{0,1:T(8,128)(2,1)} %param.5) | copy-start | bytes 98308
Sparse Core Ops, SparseCore 0:
  39.5 58.1 reduce-scatter.3
  100.1 60.4 all-gather.14
  186.4 43.3 all-gather.6
  246.6 40.4 all-gather.8
  303.9 40.4 all-gather.10
  361.3 37.8 all-gather.12
